TPU v7x, 256 devices: a whole 4x4x8 slice. The times are simulated.
256 devices in a mesh: dp: 16 (over y_hi, z), seq: 16 (over x, y_lo, core).
Axes of the slice: x: 4, y: 4 (y_hi: 2, y_lo: 2; y = y_hi * 2 + y_lo), z: 8, core: 2. Of those that a mesh axis runs over, the one named last changes fastest.
Arguments:
- queries: bfloat16 [16, 2048, 2048], P('dp', 'seq'), may hold values from -6 to 6
- key_states: bfloat16 [16, 2048, 2048], P('dp', 'seq'), may hold values from -6 to 6
- value_states: bfloat16 [16, 2048, 2048], P('dp', 'seq'), may hold values from -6 to 6
- cotangent: bfloat16 [16, 2048, 2048], P('dp', 'seq'), may hold values from -6 to 6
- filter_taps: float32 [7, 2048], replicated, may hold values from -3 to 3
Outputs:
- conv_output: bfloat16 [16, 2048, 2048], P('dp', 'seq')
- grad_queries: bfloat16 [16, 2048, 2048], P('dp', 'seq')
- grad_keys: bfloat16 [16, 2048, 2048], P('dp', 'seq')
- grad_values: bfloat16 [16, 2048, 2048], P('dp', 'seq')
- filter_gradient: float32 [7, 2048], replicated
All inputs are finite; a program needn't handle non-finite values.
Results may differ from a plain program's by a relative error of at most 0.015.
Values may be sent and summed in bfloat16 or wider, within the bound.
No kernel may reach another device: no remote copies, remote signals or barrier semaphores. Data moves between devices by JAX's collectives and lax.ppermute only.
A program may use at most 128 MiB of HBM per device.

v0:
```python
import math
import jax
import jax.numpy as jnp
import numpy as np
from jax import lax
from jax.sharding import Mesh
from jax.sharding import PartitionSpec as P

HD = 128
TAPS = 7
GROUP_HEADS = 2
SEQ = ("sc", "core")


def padded(value, width):
    peers = lax.axis_size("sc") * lax.axis_size("core")
    length = value.shape[0]
    up = [(i, (i + 1) % peers) for i in range(peers)]
    down = [(j, i) for i, j in up]
    before = lax.ppermute(value[length - width :], SEQ, up)
    after = lax.ppermute(value[:width], SEQ, down)
    return jnp.concatenate([before, value, after], axis=0)


def to_chip_rows(value):
    rows, channels = value.shape
    split = value.reshape(rows, 2, channels // 2)
    return lax.all_to_all(split, "core", 1, 0, tiled=True).reshape(2 * rows, channels // 2)


def from_chip_rows(value):
    rows2, half = value.shape
    split = value.reshape(2, rows2 // 2, 1, half)
    out = lax.all_to_all(split, "core", 0, 2, tiled=True)
    return out.reshape(rows2 // 2, 2 * half)


def on_device(queries, key_states, value_states, cotangent, filter_taps):
    tok_rows = queries.shape[1]
    channels = queries.shape[2]
    chips = lax.axis_size("sc")
    seq_total = tok_rows * chips * 2
    chip_rows = 2 * tok_rows
    half_channels = channels // 2
    head_count = half_channels // HD
    group_width = GROUP_HEADS * HD
    group_count = head_count // GROUP_HEADS
    score_scale = HD ** (-0.5)
    half_width = (TAPS - 1) // 2
    local_q = queries[0]
    local_k = key_states[0]
    local_v = value_states[0]
    local_g = cotangent[0]
    grad_pad = padded(local_g, half_width)
    grad_sum = jnp.zeros((tok_rows, channels), jnp.float32)
    for tap_index in range(TAPS):
        start_row = 2 * half_width - tap_index
        grad_sum = grad_sum + filter_taps[tap_index] * grad_pad[
            start_row : start_row + tok_rows
        ].astype(jnp.float32)
    grad_attn = grad_sum.astype(jnp.bfloat16)
    chip_q = to_chip_rows(local_q)
    chip_k = to_chip_rows(local_k)
    chip_v = to_chip_rows(local_v)
    chip_d = to_chip_rows(grad_attn)
    chip_index = lax.axis_index("sc")
    query_pos = chip_index * chip_rows + jnp.arange(chip_rows, dtype=jnp.int32)
    key_pos = jnp.arange(seq_total, dtype=jnp.int32)
    visible = query_pos[:, None] >= key_pos[None, :]
    attended_parts, grad_q_parts, key_parts, value_parts = ([], [], [], [])
    for group_index in range(group_count):
        cols = slice(group_index * group_width, (group_index + 1) * group_width)
        k_all = lax.all_gather(chip_k[:, cols], "sc", axis=0, tiled=True)
        v_all = lax.all_gather(chip_v[:, cols], "sc", axis=0, tiled=True)
        q_part = chip_q[:, cols].reshape(chip_rows, GROUP_HEADS, HD)
        d_part = chip_d[:, cols].reshape(chip_rows, GROUP_HEADS, HD)
        k_part = k_all.reshape(seq_total, GROUP_HEADS, HD)
        v_part = v_all.reshape(seq_total, GROUP_HEADS, HD)
        scores = (
            jnp.einsum("thd,uhd->htu", q_part, k_part, preferred_element_type=jnp.float32)
            * score_scale
        )
        row_top = jnp.max(jnp.where(visible, scores, -jnp.inf), -1, keepdims=True)
        raw = jnp.where(visible, jnp.exp(scores - row_top), 0.0)
        row_total = jnp.sum(raw, -1, keepdims=True)
        probs = raw / row_total
        probs_low = probs.astype(jnp.bfloat16)
        attended = jnp.einsum("htu,uhd->thd", probs_low, v_part, preferred_element_type=jnp.float32)
        attended_parts.append(attended.astype(jnp.bfloat16).reshape(chip_rows, group_width))
        dprob = jnp.einsum("thd,uhd->htu", d_part, v_part, preferred_element_type=jnp.float32)
        row_delta = jnp.sum(probs * dprob, -1, keepdims=True)
        dscore = (probs * (dprob - row_delta) * score_scale).astype(jnp.bfloat16)
        grad_q = jnp.einsum("htu,uhd->thd", dscore, k_part, preferred_element_type=jnp.float32)
        grad_q_parts.append(grad_q.astype(jnp.bfloat16).reshape(chip_rows, group_width))
        key_term = jnp.einsum("htu,thd->uhd", dscore, q_part, preferred_element_type=jnp.float32)
        value_term = jnp.einsum(
            "htu,thd->uhd", probs_low, d_part, preferred_element_type=jnp.float32
        )
        key_parts.append(
            lax.psum_scatter(
                key_term.astype(jnp.bfloat16).reshape(seq_total, group_width),
                "sc",
                scatter_dimension=0,
                tiled=True,
            )
        )
        value_parts.append(
            lax.psum_scatter(
                value_term.astype(jnp.bfloat16).reshape(seq_total, group_width),
                "sc",
                scatter_dimension=0,
                tiled=True,
            )
        )
    attn_out = from_chip_rows(jnp.concatenate(attended_parts, axis=1))
    grad_queries = from_chip_rows(jnp.concatenate(grad_q_parts, axis=1))
    grad_keys = from_chip_rows(jnp.concatenate(key_parts, axis=1))
    grad_values = from_chip_rows(jnp.concatenate(value_parts, axis=1))
    out_pad = padded(attn_out, half_width)
    conv_sum = jnp.zeros((tok_rows, channels), jnp.float32)
    filter_rows = []
    local_gf = local_g.astype(jnp.float32)
    for tap_index in range(TAPS):
        moved = out_pad[tap_index : tap_index + tok_rows].astype(jnp.float32)
        conv_sum = conv_sum + filter_taps[tap_index] * moved
        filter_rows.append(jnp.sum(moved * local_gf, 0))
    filter_gradient = lax.psum(jnp.stack(filter_rows, 0), ("dp", "sc", "core"))
    conv_output = conv_sum.astype(jnp.bfloat16)
    return (
        conv_output[None],
        grad_queries[None],
        grad_keys[None],
        grad_values[None],
        filter_gradient,
    )


def solution(mesh):
    devices = np.asarray(mesh.devices)
    dp_size, seq_size = devices.shape
    split_mesh = Mesh(devices.reshape(dp_size, seq_size // 2, 2), ("dp", "sc", "core"))
    block = P("dp", SEQ, None)
    in_specs = (block, block, block, block, P())
    out_specs = (block, block, block, block, P())
    return jax.shard_map(
        on_device, mesh=split_mesh, in_specs=in_specs, out_specs=out_specs, check_vma=False
    )
```

profile of v0, /device:TPU:1, one launch (start us, length us, event | category | flops | bytes accessed | tf_op | source)
XLA Modules:
  0.0 740.7 jit_solution(332086236696625652)
XLA Ops:
  7.2 1.4 copy.278
  8.6 7.2 all_to_all.120
  17.2 4.2 all_to_all.121
  26.6 3.9 all-to-all-start
  31.8 1.7 collective-permute-start.3
  36.2 20.8 %collective-permute-done.2 = bf16[3,2048]{0,1:T(8,128)(2,1)S(1)} collective-permute-done((bf16[3,2048]{0,1:T(8,128)(2,1)}, bf16[3,2048]{0,1:T(8,128)(2,1)S(1)}, u32[]{:S(2)}, u32[]{:S(2)}) %collective-permute-start.2) | collective-permute-done | bytes 12320 | tf_op jit(solution)/shard_map/ppermute | solution.py:21
  57.0 1.1 collective-permute-done.3
  58.1 5.9 fusion.115
  64.0 3.8 all_to_all.122
  69.5 1.5 copy.289
  71.0 34.5 %all-gather.15.cloned.1.call-done = bf16[2048,256]{1,0:T(8,128)(2,1)} async-done(((bf16[256,256]{1,0:T(8,128)(2,1)}), bf16[2048,256]{1,0:T(8,128)(2,1)}) %all-gather.15.cloned.1.call-update) | async-done | bytes 1048592 | tf_op jit(solution)/shard_map/all_gather | solution.py:74
  105.5 1.5 copy.292
  107.0 3.6 fusion.183
  110.6 5.9 fusion.180
  116.5 9.7 %convolution_convert_fusion.2 = bf16[2,2048,128]{1,2,0:T(8,128)(2,1)} fusion(bf16[256,2,128]{0,2,1:T(8,128)(2,1)} %bitcast.232, f32[2,256,2048]{2,1,0:T(8,128)} %fusion.183, f32[2,256,2048]{2,1,0:T(8,128)} %get-tuple-element.66, f32[2,256]{1,0:T(2,128)} %get-tuple-element.65), kind=kOutput, calls=%fused_computation.45 | convolution fusion | flops 276302336 | bytes 9570304 | tf_op jit(solution)/shard_map/htu,thd->uhd/dot_general | solution.py:95
  127.9 19.7 %all-gather.17.cloned.1.call-done = bf16[2048,256]{1,0:T(8,128)(2,1)} async-done(((bf16[256,256]{1,0:T(8,128)(2,1)}), bf16[2048,256]{1,0:T(8,128)(2,1)}) %all-gather.17.cloned.1.call-update) | async-done | bytes 1048592 | tf_op jit(solution)/shard_map/all_gather | solution.py:73
  147.6 2.3 copy.296
  149.9 41.5 %all-gather.19.cloned.1.call-done = bf16[2048,256]{1,0:T(8,128)(2,1)} async-done(((bf16[256,256]{1,0:T(8,128)(2,1)}), bf16[2048,256]{1,0:T(8,128)(2,1)}) %all-gather.19.cloned.1.call-update) | async-done | bytes 1048592 | tf_op jit(solution)/shard_map/all_gather | solution.py:74
  191.4 1.5 copy.299
  192.9 3.6 fusion.184
  196.5 6.5 fusion.179
  203.1 9.7 %convolution_convert_fusion.1 = bf16[2,2048,128]{1,2,0:T(8,128)(2,1)} fusion(bf16[256,2,128]{0,2,1:T(8,128)(2,1)} %bitcast.236, f32[2,256,2048]{2,1,0:T(8,128)} %fusion.184, f32[2,256,2048]{2,1,0:T(8,128)} %get-tuple-element.64, f32[2,256]{1,0:T(2,128)} %get-tuple-element.63), kind=kOutput, calls=%fused_computation.44 | convolution fusion | flops 276302336 | bytes 9570304 | tf_op jit(solution)/shard_map/htu,thd->uhd/dot_general | solution.py:95
  214.6 19.3 %all-gather.21.cloned.1.call-done = bf16[2048,256]{1,0:T(8,128)(2,1)} async-done(((bf16[256,256]{1,0:T(8,128)(2,1)}), bf16[2048,256]{1,0:T(8,128)(2,1)}) %all-gather.21.cloned.1.call-update) | async-done | bytes 1048592 | tf_op jit(solution)/shard_map/all_gather | solution.py:73
  233.9 2.3 copy.303
  236.1 41.4 %all-gather.23.cloned.1.call-done = bf16[2048,256]{1,0:T(8,128)(2,1)} async-done(((bf16[256,256]{1,0:T(8,128)(2,1)}), bf16[2048,256]{1,0:T(8,128)(2,1)}) %all-gather.23.cloned.1.call-update) | async-done | bytes 1048592 | tf_op jit(solution)/shard_map/all_gather | solution.py:74
  277.5 2.3 copy.306
  279.8 3.9 fusion.185
  283.7 6.5 fusion.178
  290.2 9.7 %convolution_convert_fusion = bf16[2,2048,128]{1,2,0:T(8,128)(2,1)} fusion(bf16[256,2,128]{0,2,1:T(8,128)(2,1)} %bitcast.238, f32[2,256,2048]{2,1,0:T(8,128)} %fusion.185, f32[2,256,2048]{2,1,0:T(8,128)} %get-tuple-element.62, f32[2,256]{1,0:T(2,128)} %get-tuple-element.61), kind=kOutput, calls=%fused_computation.43 | convolution fusion | flops 276302336 | bytes 9570304 | tf_op jit(solution)/shard_map/htu,thd->uhd/dot_general | solution.py:95
  301.1 18.5 %all-gather.9.cloned.1.call-done = bf16[2048,256]{1,0:T(8,128)(2,1)} async-done(((bf16[256,256]{1,0:T(8,128)(2,1)}), bf16[2048,256]{1,0:T(8,128)(2,1)}) %all-gather.9.cloned.1.call-update) | async-done | bytes 1048592 | tf_op jit(solution)/shard_map/all_gather | solution.py:73
  319.6 2.3 copy.280
  321.9 42.0 %all-gather.11.cloned.1.call-done = bf16[2048,256]{1,0:T(8,128)(2,1)} async-done(((bf16[256,256]{1,0:T(8,128)(2,1)}), bf16[2048,256]{1,0:T(8,128)(2,1)}) %all-gather.11.cloned.1.call-update) | async-done | bytes 1048592 | tf_op jit(solution)/shard_map/all_gather | solution.py:74
  363.8 2.3 copy.285
  366.1 3.9 fusion.182
  370.0 6.0 fusion.181
  376.0 9.6 %convolution_convert_fusion.3 = bf16[2,2048,128]{1,2,0:T(8,128)(2,1)} fusion(bf16[256,2,128]{0,2,1:T(8,128)(2,1)S(1)} %bitcast.234, f32[2,256,2048]{2,1,0:T(8,128)} %fusion.182, f32[2,256,2048]{2,1,0:T(8,128)} %get-tuple-element.68, f32[2,256]{1,0:T(2,128)S(1)} %get-tuple-element.67), kind=kOutput, calls=%fused_computation.46 | convolution fusion | flops 276302336 | bytes 9570304 | tf_op jit(solution)/shard_map/htu,thd->uhd/dot_general | solution.py:95
  385.8 3.8 convolution_convert_fusion.6
  389.6 3.7 convolution_convert_fusion.5
  393.4 3.0 fusion.101
  396.6 8.2 %fusion.91 = bf16[256,2,128]{2,0,1:T(8,128)(2,1)S(1)} fusion(bf16[2048,2,128]{0,2,1:T(8,128)(2,1)} %bitcast.215, f32[2,256,2048]{2,1,0:T(8,128)} %fusion.183, f32[2,256,2048]{2,1,0:T(8,128)} %get-tuple-element.66, f32[2,256]{1,0:T(2,128)S(1)} %copy-done.23), kind=kOutput, calls=%fused_computation.111 | convolution fusion | flops 275843584 | bytes 9570304 | tf_op jit(solution)/shard_map/htu,uhd->thd/dot_general | solution.py:93
  405.1 3.0 fusion.102
  408.4 3.8 convolution_convert_fusion.4
  412.7 7.9 %fusion.94 = bf16[256,2,128]{2,0,1:T(8,128)(2,1)S(1)} fusion(bf16[2048,2,128]{0,2,1:T(8,128)(2,1)S(1)} %bitcast.217, f32[2,256,2048]{2,1,0:T(8,128)} %fusion.184, f32[2,256,2048]{2,1,0:T(8,128)} %get-tuple-element.64, f32[2,256]{1,0:T(2,128)S(1)} %copy-done.24), kind=kOutput, calls=%fused_computation.112 | convolution fusion | flops 275843584 | bytes 9570304 | tf_op jit(solution)/shard_map/htu,uhd->thd/dot_general | solution.py:93
  420.8 3.0 fusion.103
  424.1 4.0 convolution_convert_fusion.7
  429.3 8.1 %fusion.97 = bf16[256,2,128]{2,0,1:T(8,128)(2,1)S(1)} fusion(bf16[2048,2,128]{0,2,1:T(8,128)(2,1)S(1)} %bitcast.219, f32[2,256,2048]{2,1,0:T(8,128)} %fusion.185, f32[2,256,2048]{2,1,0:T(8,128)} %get-tuple-element.62, f32[2,256]{1,0:T(2,128)} %get-tuple-element.61), kind=kOutput, calls=%fused_computation.113 | convolution fusion | flops 275843584 | bytes 9570304 | tf_op jit(solution)/shard_map/htu,uhd->thd/dot_general | solution.py:93
  437.9 8.0 %fusion.88 = bf16[256,2,128]{2,0,1:T(8,128)(2,1)S(1)} fusion(bf16[2048,2,128]{0,2,1:T(8,128)(2,1)S(1)} %bitcast.221, f32[2,256,2048]{2,1,0:T(8,128)} %fusion.182, f32[2,256,2048]{2,1,0:T(8,128)} %get-tuple-element.68, f32[2,256]{1,0:T(2,128)} %copy-done.26), kind=kOutput, calls=%fused_computation.110 | convolution fusion | flops 275843584 | bytes 9570304 | tf_op jit(solution)/shard_map/htu,uhd->thd/dot_general | solution.py:93
  447.1 8.7 %all-to-all-start.3 = ((bf16[2,128,1,1024]{3,1,2,0:T(8,128)(2,1)}), bf16[2,128,1,1024]{3,1,2,0:T(8,128)(2,1)S(1)}, u32[]{:S(2)}, u32[]{:S(2)}) async-start(bf16[2,128,1,1024]{3,1,2,0:T(8,128)(2,1)} %maximum_bitcast_fusion), calls=%async_computation.3 | async-start | bytes 1048576 | tf_op jit(solution)/shard_map/all_to_all | solution.py:34
  457.1 3.9 all-to-all-start.5
  463.0 1.0 copy.347
  464.4 7.4 collective-permute-done.1
  471.8 3.8 fusion.139
  476.5 3.4 fusion.121
  480.0 81.5 %psum.7 = f32[7,2048]{1,0:T(8,128)} all-reduce(f32[7,2048]{1,0:T(8,128)S(1)} %stack.31), channel_id=1, replica_groups=mesh['dp'=16,'sc'=8,'core'=2] {'dp','sc','core'}, use_global_device_ids=true, to_apply=%region_27.28 | all-reduce | flops 14336 | bytes 114688 | tf_op jit(solution)/shard_map/psum | solution.py:127
  561.6 1.1 pad_maximum_fusion.4
  563.0 23.9 %reduce-scatter.19.cloned.1.call-done = bf16[256,256]{0,1:T(8,128)(2,1)} async-done(((bf16[2048,256]{0,1:T(8,128)(2,1)}), bf16[256,256]{0,1:T(8,128)(2,1)}) %reduce-scatter.19.cloned.1.call-update) | async-done | bytes 131088 | tf_op jit(solution)/shard_map/reduce_scatter | solution.py:108
  586.8 43.3 %reduce-scatter.21.cloned.1.call-done = bf16[256,256]{0,1:T(8,128)(2,1)} async-done(((bf16[2048,256]{0,1:T(8,128)(2,1)}), bf16[256,256]{0,1:T(8,128)(2,1)}) %reduce-scatter.21.cloned.1.call-update) | async-done | bytes 131088 | tf_op jit(solution)/shard_map/reduce_scatter | solution.py:108
  630.1 43.4 %reduce-scatter.23.cloned.1.call-done = bf16[256,256]{0,1:T(8,128)(2,1)} async-done(((bf16[2048,256]{0,1:T(8,128)(2,1)}), bf16[256,256]{0,1:T(8,128)(2,1)}) %reduce-scatter.23.cloned.1.call-update) | async-done | bytes 131088 | tf_op jit(solution)/shard_map/reduce_scatter | solution.py:108
  673.5 43.4 %reduce-scatter.17.cloned.1.call-done = bf16[256,256]{0,1:T(8,128)(2,1)} async-done(((bf16[2048,256]{0,1:T(8,128)(2,1)}), bf16[256,256]{0,1:T(8,128)(2,1)}) %reduce-scatter.17.cloned.1.call-update) | async-done | bytes 131088 | tf_op jit(solution)/shard_map/reduce_scatter | solution.py:108
  716.9 1.1 pad_maximum_fusion.5
  718.3 9.0 %all_to_all.123 = bf16[2,128,1,1024]{3,1,2,0:T(8,128)(2,1)S(1)} all-to-all(bf16[2,128,1,1024]{3,1,2,0:T(8,128)(2,1)S(1)} %bitcast.199), channel_id=1, replica_groups=mesh['dp'=16,'sc'=8,'core'=2] {'core'}, dimensions={0} | all-to-all | bytes 1048576 | tf_op jit(solution)/shard_map/all_to_all | solution.py:34
  727.5 1.0 copy.349
  728.5 4.1 all_to_all.124
  733.0 1.0 copy.348
  (155 shorter events, 27.4 us)
Async XLA Ops:
  7.2 9.7 %copy-start.6 = (bf16[1,128,2048]{2,1,0:T(8,128)(2,1)S(1)}, bf16[1,128,2048]{2,1,0:T(8,128)(2,1)}, u32[]{:S(2)}) copy-start(bf16[1,128,2048]{2,1,0:T(8,128)(2,1)} %param.7) | copy-start | bytes 1572868
  7.2 62.3 %all-gather.13.cloned.1.call-start = ((), (), s32[]{:S(2)}) async-start(), calls=%async_computation.18 | async-start | bytes 1179648 | tf_op jit(solution)/shard_map/all_gather | solution.py:73
  8.6 17.0 %copy-start.7 = (bf16[1,128,2048]{2,1,0:T(8,128)(2,1)S(1)}, bf16[1,128,2048]{2,1,0:T(8,128)(2,1)}, u32[]{:S(2)}) copy-start(bf16[1,128,2048]{2,1,0:T(8,128)(2,1)} %param.5) | copy-start | bytes 1572868
  16.0 14.5 %copy-start.8 = (bf16[1,128,2048]{2,1,0:T(8,128)(2,1)S(1)}, bf16[1,128,2048]{2,1,0:T(8,128)(2,1)}, u32[]{:S(2)}) copy-start(bf16[1,128,2048]{2,1,0:T(8,128)(2,1)} %param.8) | copy-start | bytes 1572868
  16.8 88.7 %all-gather.15.cloned.1.call-start = ((), (), s32[]{:S(2)}) async-start(), calls=%async_computation.19 | async-start | bytes 1179648 | tf_op jit(solution)/shard_map/all_gather | solution.py:74
  21.3 12.2 %copy-start.21 = (f32[7,2048]{1,0:T(8,128)S(1)}, f32[7,2048]{1,0:T(8,128)}, u32[]{:S(2)}) copy-start(f32[7,2048]{1,0:T(8,128)} %param.9) | copy-start | bytes 172036
  22.4 125.3 %all-gather.17.cloned.1.call-start = ((), (), s32[]{:S(2)}) async-start(), calls=%async_computation.20 | async-start | bytes 1179648 | tf_op jit(solution)/shard_map/all_gather | solution.py:73
  23.1 168.3 %all-gather.19.cloned.1.call-start = ((), (), s32[]{:S(2)}) async-start(), calls=%async_computation.21 | async-start | bytes 1179648 | tf_op jit(solution)/shard_map/all_gather | solution.py:74
  23.7 210.2 %all-gather.21.cloned.1.call-start = ((), (), s32[]{:S(2)}) async-start(), calls=%async_computation.22 | async-start | bytes 1179648 | tf_op jit(solution)/shard_map/all_gather | solution.py:73
  24.3 253.2 %all-gather.23.cloned.1.call-start = ((), (), s32[]{:S(2)}) async-start(), calls=%async_computation.23 | async-start | bytes 1179648 | tf_op jit(solution)/shard_map/all_gather | solution.py:74
  24.8 294.7 %all-gather.9.cloned.1.call-start = ((), (), s32[]{:S(2)}) async-start(), calls=%async_computation.16 | async-start | bytes 1179648 | tf_op jit(solution)/shard_map/all_gather | solution.py:73
  26.6 8.0 %all-to-all-start = ((bf16[128,2,1024]{0,2,1:T(8,128)(2,1)}), bf16[128,2,1024]{0,2,1:T(8,128)(2,1)S(1)}, u32[]{:S(2)}, u32[]{:S(2)}) async-start(bf16[128,2,1024]{0,2,1:T(8,128)(2,1)} %bitcast.1), calls=%async_computation | async-start | bytes 1048576 | tf_op jit(solution)/shard_map/all_to_all | solution.py:28
  30.5 333.4 %all-gather.11.cloned.1.call-start = ((), (), s32[]{:S(2)}) async-start(), calls=%async_computation.17 | async-start | bytes 1179648 | tf_op jit(solution)/shard_map/all_gather | solution.py:74
  31.7 25.3 %collective-permute-start.2 = (bf16[3,2048]{0,1:T(8,128)(2,1)}, bf16[3,2048]{0,1:T(8,128)(2,1)S(1)}, u32[]{:S(2)}, u32[]{:S(2)}) collective-permute-start(bf16[3,2048]{0,1:T(8,128)(2,1)} %get-tuple-element.38), channel_id=1, source_target_pairs={{1,0},{2,1},{3,2},{4,3},{5,4},{6,5},{7,6},{8,7},{9,8},{10,9},{11,1... | collective-permute-start | bytes 36872 | tf_op jit(solution)/shard_map/ppermute | solution.py:21
  31.8 26.3 %collective-permute-start.3 = (bf16[3,2048]{0,1:T(8,128)(2,1)S(1)}, bf16[3,2048]{0,1:T(8,128)(2,1)}, u32[]{:S(2)}, u32[]{:S(2)}) collective-permute-start(bf16[3,2048]{0,1:T(8,128)(2,1)S(1)} %get-tuple-element.39), channel_id=1, source_target_pairs={{0,1},{1,2},{2,3},{3,4},{4,5},{5,6},{6,7},{7,8},{8,9},{9,10},{10,1... | collective-permute-start | bytes 36872 | tf_op jit(solution)/shard_map/ppermute | solution.py:20
  33.5 528.1 %reduce-scatter.11.cloned.1.call-start = ((), (), s32[]{:S(2)}) async-start(), calls=%async_computation.25 | async-start | bytes 1179648 | tf_op jit(solution)/shard_map/reduce_scatter | solution.py:100
  71.0 45.5 %copy-start.2 = (bf16[2048,256]{0,1:T(8,128)(2,1)}, bf16[2048,256]{0,1:T(8,128)(2,1)S(1)}, u32[]{:S(2)}) copy-start(bf16[2048,256]{0,1:T(8,128)(2,1)S(1)} %copy.289) | copy-start | bytes 3145732
  116.5 9.9 %copy-start.9 = (bf16[256,256]{1,0:T(8,128)(2,1)S(1)}, bf16[256,256]{1,0:T(8,128)(2,1)}, u32[]{:S(2)}) copy-start(bf16[256,256]{1,0:T(8,128)(2,1)} %get-tuple-element.48) | copy-start | bytes 393220
  116.5 10.7 %copy-start.10 = (bf16[256,256]{1,0:T(8,128)(2,1)S(1)}, bf16[256,256]{1,0:T(8,128)(2,1)}, u32[]{:S(2)}) copy-start(bf16[256,256]{1,0:T(8,128)(2,1)} %get-tuple-element.36) | copy-start | bytes 393220
  126.1 435.4 %reduce-scatter.13.cloned.1.call-start = ((), (), s32[]{:S(2)}) async-start(), calls=%async_computation.26 | async-start | bytes 1179648 | tf_op jit(solution)/shard_map/reduce_scatter | solution.py:100
  212.8 348.8 %reduce-scatter.15.cloned.1.call-start = ((), (), s32[]{:S(2)}) async-start(), calls=%async_computation.27 | async-start | bytes 1179648 | tf_op jit(solution)/shard_map/reduce_scatter | solution.py:100
  300.0 261.6 %reduce-scatter.9.cloned.1.call-start = ((), (), s32[]{:S(2)}) async-start(), calls=%async_computation.24 | async-start | bytes 1179648 | tf_op jit(solution)/shard_map/reduce_scatter | solution.py:100
  301.1 68.9 %copy-start.13 = (bf16[256,256]{0,1:T(8,128)(2,1)}, bf16[256,256]{0,1:T(8,128)(2,1)S(1)}, u32[]{:S(2)}) copy-start(bf16[256,256]{0,1:T(8,128)(2,1)S(1)} %copy.319) | copy-start | bytes 393220
  321.9 48.2 %copy-start.15 = (bf16[256,256]{0,1:T(8,128)(2,1)S(1)}, bf16[256,256]{0,1:T(8,128)(2,1)}, u32[]{:S(2)}) copy-start(bf16[256,256]{0,1:T(8,128)(2,1)} %copy.277) | copy-start | bytes 393220
  376.0 9.6 %copy-start.26 = (f32[2,256]{1,0:T(2,128)}, f32[2,256]{1,0:T(2,128)S(1)}, u32[]{:S(2)}) copy-start(f32[2,256]{1,0:T(2,128)S(1)} %get-tuple-element.67) | copy-start | bytes 6148
  376.0 9.7 %copy-start.11 = (bf16[256,256]{0,1:T(8,128)(2,1)S(1)}, bf16[256,256]{0,1:T(8,128)(2,1)}, u32[]{:S(2)}) copy-start(bf16[256,256]{0,1:T(8,128)(2,1)} %copy.324) | copy-start | bytes 393220
  376.0 9.7 %copy-start.23 = (f32[2,256]{1,0:T(2,128)S(1)}, f32[2,256]{1,0:T(2,128)}, u32[]{:S(2)}) copy-start(f32[2,256]{1,0:T(2,128)} %get-tuple-element.65) | copy-start | bytes 6148
  385.7 3.9 copy-start.12
  385.7 3.9 copy-start.24
  385.7 201.1 %reduce-scatter.19.cloned.1.call-start = ((), (), s32[]{:S(2)}) async-start(), calls=%async_computation.29 | async-start | bytes 1179648 | tf_op jit(solution)/shard_map/reduce_scatter | solution.py:108
  389.5 240.6 %reduce-scatter.21.cloned.1.call-start = ((), (), s32[]{:S(2)}) async-start(), calls=%async_computation.30 | async-start | bytes 1179648 | tf_op jit(solution)/shard_map/reduce_scatter | solution.py:108
  393.4 280.1 %reduce-scatter.23.cloned.1.call-start = ((), (), s32[]{:S(2)}) async-start(), calls=%async_computation.31 | async-start | bytes 1179648 | tf_op jit(solution)/shard_map/reduce_scatter | solution.py:108
  405.1 3.3 copy-start.25
  408.4 4.3 copy-start.3
  412.2 8.6 %copy-start = (bf16[2048,256]{0,1:T(8,128)(2,1)S(1)}, bf16[2048,256]{0,1:T(8,128)(2,1)}, u32[]{:S(2)}) copy-start(bf16[2048,256]{0,1:T(8,128)(2,1)} %copy.306) | copy-start | bytes 3145732
  412.2 304.7 %reduce-scatter.17.cloned.1.call-start = ((), (), s32[]{:S(2)}) async-start(), calls=%async_computation.28 | async-start | bytes 1179648 | tf_op jit(solution)/shard_map/reduce_scatter | solution.py:108
  420.8 3.3 copy-start.14
  420.8 3.3 copy-start.27
  424.1 4.0 copy-start.1
  424.1 4.0 copy-start.22
  428.1 1.2 copy-start.4
  429.3 8.6 %copy-start.5 = (bf16[2048,256]{0,1:T(8,128)(2,1)S(1)}, bf16[2048,256]{0,1:T(8,128)(2,1)}, u32[]{:S(2)}) copy-start(bf16[2048,256]{0,1:T(8,128)(2,1)} %copy.280) | copy-start | bytes 3145732
  447.1 10.0 %all-to-all-start.3 = ((bf16[2,128,1,1024]{3,1,2,0:T(8,128)(2,1)}), bf16[2,128,1,1024]{3,1,2,0:T(8,128)(2,1)S(1)}, u32[]{:S(2)}, u32[]{:S(2)}) async-start(bf16[2,128,1,1024]{3,1,2,0:T(8,128)(2,1)} %maximum_bitcast_fusion), calls=%async_computation.3 | async-start | bytes 1048576 | tf_op jit(solution)/shard_map/all_to_all | solution.py:34
  456.6 15.2 %copy-start.16 = (f32[1,2048]{1,0:T(1,128)S(1)}, f32[1,2048]{1,0:T(1,128)}, u32[]{:S(2)}) copy-start(f32[1,2048]{1,0:T(1,128)} %get-tuple-element.56) | copy-start | bytes 24580
  456.6 15.2 %copy-start.17 = (f32[1,2048]{1,0:T(1,128)S(1)}, f32[1,2048]{1,0:T(1,128)}, u32[]{:S(2)}) copy-start(f32[1,2048]{1,0:T(1,128)} %get-tuple-element.57) | copy-start | bytes 24580
  456.6 15.2 %copy-start.18 = (f32[1,2048]{1,0:T(1,128)S(1)}, f32[1,2048]{1,0:T(1,128)}, u32[]{:S(2)}) copy-start(f32[1,2048]{1,0:T(1,128)} %get-tuple-element.58) | copy-start | bytes 24580
  456.6 15.2 %copy-start.19 = (f32[1,2048]{1,0:T(1,128)S(1)}, f32[1,2048]{1,0:T(1,128)}, u32[]{:S(2)}) copy-start(f32[1,2048]{1,0:T(1,128)} %get-tuple-element.59) | copy-start | bytes 24580
  456.6 15.2 %copy-start.20 = (f32[1,2048]{1,0:T(1,128)S(1)}, f32[1,2048]{1,0:T(1,128)}, u32[]{:S(2)}) copy-start(f32[1,2048]{1,0:T(1,128)} %get-tuple-element.60) | copy-start | bytes 24580
  457.1 5.6 all-to-all-start.5
  461.7 2.4 collective-permute-start
  461.7 10.0 %collective-permute-start.1 = (bf16[3,2048]{0,1:T(8,128)(2,1)S(1)}, bf16[3,2048]{0,1:T(8,128)(2,1)S(1)}, u32[]{:S(2)}, u32[]{:S(2)}) collective-permute-start(bf16[3,2048]{0,1:T(8,128)(2,1)S(1)} %bitcast.222), channel_id=1, source_target_pairs={{1,0},{2,1},{3,2},{4,3},{5,4},{6,5},{7,6},{8,7},{9,8},{10,9},{11,1... | collective-permute-start | bytes 36872 | tf_op jit(solution)/shard_map/ppermute | solution.py:21
Sparse Core Ops, SparseCore 0:
  16.9 45.7 all-gather.12
  64.6 40.9 all-gather.14
  107.3 40.2 all-gather.16
  149.3 42.1 all-gather.18
  193.0 40.7 all-gather.20
  236.1 41.3 all-gather.22
  279.3 40.2 all-gather.8
  321.9 41.8 all-gather.10
  366.4 41.0 reduce-scatter.10
  409.8 41.1 reduce-scatter.12
  453.5 44.8 reduce-scatter.14
  500.8 42.3 reduce-scatter.8
  545.8 41.0 reduce-scatter.18
  589.2 40.8 reduce-scatter.20
  632.5 40.9 reduce-scatter.22
  675.9 40.9 reduce-scatter.16
where the time goes:
time: 750 us; the launch traced here: 741 us
  waiting for transfers between devices  404 us (54%)
  matrix products  136 us (18%)
  blocking collectives  110 us (15%)
  local copies, waits for them, and re-layouts  38.6 us (5%)
  starting transfers between devices  20.2 us (3%)
  other arithmetic  17.8 us (2%)
  between operations  14.8 us (2%)
    all_gather x4, waiting for transfers between devices, on_device(): v_all = lax.all_gather(chip_v[:, cols], 'sc', axis=0, tiled=True)  159 us
    reduce_scatter x4, waiting for transfers between devices, on_device(): lax.psum_scatter(value_term.astype(jnp.bfloat16).reshape(seq_total, group...  154 us
    psum x1, blocking collectives, on_device(): filter_gradient = lax.psum(jnp.stack(filter_rows, 0), ('dp', 'sc', 'core'))  81.5 us
    all_gather x4, waiting for transfers between devices, on_device(): k_all = lax.all_gather(chip_k[:, cols], 'sc', axis=0, tiled=True)  57.5 us
    dot_general x4, matrix products, on_device(): jnp.einsum('htu,thd->uhd', dscore, q_part, preferred_element_type=jnp.flo...  38.7 us
    dot_general x4, matrix products, on_device(): jnp.einsum('htu,uhd->thd', dscore, k_part, preferred_element_type=jnp.flo...  32.2 us
    ppermute x2, waiting for transfers between devices, padded(): after = lax.ppermute(value[:width], SEQ, down)  28.2 us
    sub x4, matrix products, on_device(): raw = jnp.where(visible, jnp.exp(scores - row_top), 0.0)  24.9 us
  transfers between devices with their start and end apart: 23, of which 15 were waited for; matrix products, arithmetic and copies ran while one was open for 25% of the time, Pallas kernels for 0%

commit v1 on v0

--- a/solution.py
+++ b/solution.py
@@ -25,7 +25,10 @@
 def to_chip_rows(value):
     rows, channels = value.shape
     split = value.reshape(rows, 2, channels // 2)
-    return lax.all_to_all(split, "core", 1, 0, tiled=True).reshape(2 * rows, channels // 2)
+    return jnp.concatenate(
+        lax.all_to_all(jnp.stack(jnp.split(split, lax.axis_size("core"), axis=1)), "core", 0, 0),
+        axis=0,
+    ).reshape(2 * rows, channels // 2)
 
 
 def from_chip_rows(value):

time: 750 us -> 748 us (level)
    ppermute x2, waiting for transfers between devices: 1.06 us -> 16 us  [padded(): before = lax.ppermute(value[length - width:], SEQ, up)]
    reduce_scatter x4, waiting for transfers between devices: 154 us -> 143 us  [on_device(): lax.psum_scatter(value_term.astype(jnp.bfloat16).reshape(seq_total, group...]
  transfers between devices with their start and end apart: 23 -> 23, of which waited for: 15 -> 16; matrix products, arithmetic and copies ran while one was open for 25% -> 25% of each run, Pallas kernels for 0% -> 0%
where the time goes in v1:
time: 748 us; the launch traced here: 739 us
  waiting for transfers between devices  405 us (54%)
  matrix products  135 us (18%)
  blocking collectives  105 us (14%)
  local copies, waits for them, and re-layouts  34.1 us (5%)
  other arithmetic  23.2 us (3%)
  starting transfers between devices  20.4 us (3%)
  between operations  15.2 us (2%)
    all_gather x4, waiting for transfers between devices, on_device(): v_all = lax.all_gather(chip_v[:, cols], 'sc', axis=0, tiled=True)  156 us
    reduce_scatter x4, waiting for transfers between devices, on_device(): lax.psum_scatter(value_term.astype(jnp.bfloat16).reshape(seq_total, group...  143 us
    psum x1, blocking collectives, on_device(): filter_gradient = lax.psum(jnp.stack(filter_rows, 0), ('dp', 'sc', 'core'))  77 us
    all_gather x4, waiting for transfers between devices, on_device(): k_all = lax.all_gather(chip_k[:, cols], 'sc', axis=0, tiled=True)  60.9 us
    dot_general x4, matrix products, on_device(): jnp.einsum('htu,thd->uhd', dscore, q_part, preferred_element_type=jnp.flo...  38.7 us
    dot_general x4, matrix products, on_device(): jnp.einsum('htu,uhd->thd', dscore, k_part, preferred_element_type=jnp.flo...  32.6 us
    sub x4, matrix products, on_device(): raw = jnp.where(visible, jnp.exp(scores - row_top), 0.0)  26.2 us
    ppermute x2, waiting for transfers between devices, padded(): after = lax.ppermute(value[:width], SEQ, down)  25.9 us
  transfers between devices with their start and end apart: 23, of which 16 were waited for; matrix products, arithmetic and copies ran while one was open for 25% of the time, Pallas kernels for 0%

profile of v1, /device:TPU:1, one launch (start us, length us, event | category | flops | bytes accessed | tf_op | source)
XLA Modules:
  0.0 738.6 jit_solution(14710767202516883610)
XLA Ops:
  7.2 1.4 copy.247
  8.7 7.0 all_to_all.80
  17.3 4.3 all_to_all.81
  27.0 3.9 all-to-all-start.1
  32.2 1.7 collective-permute-start.3
  34.6 1.2 iota_compare_fusion
  37.4 20.8 %collective-permute-done.2 = bf16[3,2048]{0,1:T(8,128)(2,1)S(1)} collective-permute-done((bf16[3,2048]{0,1:T(8,128)(2,1)}, bf16[3,2048]{0,1:T(8,128)(2,1)S(1)}, u32[]{:S(2)}, u32[]{:S(2)}) %collective-permute-start.2) | collective-permute-done | bytes 12320 | tf_op jit(solution)/shard_map/ppermute | solution.py:21
  59.2 5.9 fusion.115
  65.2 3.8 all_to_all.82
  70.7 1.5 copy.256
  72.2 32.7 %all-gather.13.cloned.1.call-done = bf16[2048,256]{1,0:T(8,128)(2,1)} async-done(((bf16[256,256]{1,0:T(8,128)(2,1)}), bf16[2048,256]{1,0:T(8,128)(2,1)}) %all-gather.13.cloned.1.call-update) | async-done | bytes 1048592 | tf_op jit(solution)/shard_map/all_gather | solution.py:77
  104.9 1.5 copy.254
  106.4 3.6 fusion.182
  110.0 6.2 fusion.179
  116.2 9.7 %convolution_convert_fusion.6 = bf16[2,128,2048]{2,1,0:T(8,128)(2,1)} fusion(bf16[256,2,128]{0,2,1:T(8,128)(2,1)} %bitcast.242, f32[2,256,2048]{2,1,0:T(8,128)} %fusion.182, f32[2,256,2048]{2,1,0:T(8,128)} %get-tuple-element.74, f32[2,256]{1,0:T(2,128)} %get-tuple-element.73), kind=kOutput, calls=%fused_computation.49 | convolution fusion | flops 276302336 | bytes 9570304 | tf_op jit(solution)/shard_map/htu,thd->uhd/dot_general | solution.py:98
  127.7 20.1 %all-gather.19.cloned.1.call-done = bf16[2048,256]{1,0:T(8,128)(2,1)} async-done(((bf16[256,256]{1,0:T(8,128)(2,1)}), bf16[2048,256]{1,0:T(8,128)(2,1)}) %all-gather.19.cloned.1.call-update) | async-done | bytes 1048592 | tf_op jit(solution)/shard_map/all_gather | solution.py:76
  147.8 2.3 copy.261
  150.1 40.8 %all-gather.17.cloned.1.call-done = bf16[2048,256]{1,0:T(8,128)(2,1)} async-done(((bf16[256,256]{1,0:T(8,128)(2,1)}), bf16[2048,256]{1,0:T(8,128)(2,1)}) %all-gather.17.cloned.1.call-update) | async-done | bytes 1048592 | tf_op jit(solution)/shard_map/all_gather | solution.py:77
  190.9 1.5 copy.259
  192.4 3.8 fusion.183
  196.1 6.8 fusion.178
  202.9 9.7 %convolution_convert_fusion.5 = bf16[2,128,2048]{2,1,0:T(8,128)(2,1)} fusion(bf16[256,2,128]{0,2,1:T(8,128)(2,1)} %bitcast.246, f32[2,256,2048]{2,1,0:T(8,128)} %fusion.183, f32[2,256,2048]{2,1,0:T(8,128)} %get-tuple-element.72, f32[2,256]{1,0:T(2,128)} %get-tuple-element.71), kind=kOutput, calls=%fused_computation.48 | convolution fusion | flops 276302336 | bytes 9570304 | tf_op jit(solution)/shard_map/htu,thd->uhd/dot_general | solution.py:98
  213.6 19.9 %all-gather.23.cloned.1.call-done = bf16[2048,256]{1,0:T(8,128)(2,1)} async-done(((bf16[256,256]{1,0:T(8,128)(2,1)}), bf16[2048,256]{1,0:T(8,128)(2,1)}) %all-gather.23.cloned.1.call-update) | async-done | bytes 1048592 | tf_op jit(solution)/shard_map/all_gather | solution.py:76
  233.5 2.3 copy.266
  235.7 40.9 %all-gather.21.cloned.1.call-done = bf16[2048,256]{1,0:T(8,128)(2,1)} async-done(((bf16[256,256]{1,0:T(8,128)(2,1)}), bf16[2048,256]{1,0:T(8,128)(2,1)}) %all-gather.21.cloned.1.call-update) | async-done | bytes 1048592 | tf_op jit(solution)/shard_map/all_gather | solution.py:77
  276.6 1.5 copy.264
  278.1 2.7 fusion.184
  280.9 6.9 fusion.177
  287.8 9.7 %convolution_convert_fusion.4 = bf16[2,128,2048]{2,1,0:T(8,128)(2,1)} fusion(bf16[256,2,128]{0,2,1:T(8,128)(2,1)} %bitcast.248, f32[2,256,2048]{2,1,0:T(8,128)} %fusion.184, f32[2,256,2048]{2,1,0:T(8,128)} %get-tuple-element.70, f32[2,256]{1,0:T(2,128)} %get-tuple-element.69), kind=kOutput, calls=%fused_computation.47 | convolution fusion | flops 276302336 | bytes 9570304 | tf_op jit(solution)/shard_map/htu,thd->uhd/dot_general | solution.py:98
  298.6 20.9 %all-gather.11.cloned.1.call-done = bf16[2048,256]{1,0:T(8,128)(2,1)} async-done(((bf16[256,256]{1,0:T(8,128)(2,1)}), bf16[2048,256]{1,0:T(8,128)(2,1)}) %all-gather.11.cloned.1.call-update) | async-done | bytes 1048592 | tf_op jit(solution)/shard_map/all_gather | solution.py:76
  319.5 2.3 copy.251
  321.8 41.3 %all-gather.9.cloned.1.call-done = bf16[2048,256]{1,0:T(8,128)(2,1)} async-done(((bf16[256,256]{1,0:T(8,128)(2,1)}), bf16[2048,256]{1,0:T(8,128)(2,1)}) %all-gather.9.cloned.1.call-update) | async-done | bytes 1048592 | tf_op jit(solution)/shard_map/all_gather | solution.py:77
  363.0 1.5 copy.241
  364.5 2.7 fusion.181
  367.2 6.3 fusion.180
  373.5 9.6 %convolution_convert_fusion.7 = bf16[2,128,2048]{2,1,0:T(8,128)(2,1)} fusion(bf16[256,2,128]{0,2,1:T(8,128)(2,1)S(1)} %bitcast.244, f32[2,256,2048]{2,1,0:T(8,128)} %fusion.181, f32[2,256,2048]{2,1,0:T(8,128)} %get-tuple-element.76, f32[2,256]{1,0:T(2,128)S(1)} %get-tuple-element.75), kind=kOutput, calls=%fused_computation.50 | convolution fusion | flops 276302336 | bytes 9570304 | tf_op jit(solution)/shard_map/htu,thd->uhd/dot_general | solution.py:98
  383.2 3.7 convolution_convert_fusion.2
  387.2 3.7 convolution_convert_fusion.1
  391.0 3.1 fusion.101
  394.2 8.3 %fusion.91 = bf16[256,2,128]{0,2,1:T(8,128)(2,1)S(1)} fusion(bf16[2048,2,128]{0,2,1:T(8,128)(2,1)} %bitcast.225, f32[2,256,2048]{2,1,0:T(8,128)} %fusion.182, f32[2,256,2048]{2,1,0:T(8,128)} %get-tuple-element.74, f32[2,256]{1,0:T(2,128)S(1)} %copy-done.27), kind=kOutput, calls=%fused_computation.111 | convolution fusion | flops 275843584 | bytes 9570304 | tf_op jit(solution)/shard_map/htu,uhd->thd/dot_general | solution.py:96
  402.6 3.1 fusion.102
  405.8 3.7 convolution_convert_fusion
  409.9 8.1 %fusion.94 = bf16[256,2,128]{0,2,1:T(8,128)(2,1)S(1)} fusion(bf16[2048,2,128]{0,2,1:T(8,128)(2,1)} %bitcast.228, f32[2,256,2048]{2,1,0:T(8,128)} %fusion.183, f32[2,256,2048]{2,1,0:T(8,128)} %get-tuple-element.72, f32[2,256]{1,0:T(2,128)S(1)} %copy-done.28), kind=kOutput, calls=%fused_computation.112 | convolution fusion | flops 275843584 | bytes 9570304 | tf_op jit(solution)/shard_map/htu,uhd->thd/dot_general | solution.py:96
  418.1 3.1 fusion.103
  421.4 3.9 convolution_convert_fusion.3
  426.5 7.9 %fusion.97 = bf16[256,2,128]{0,2,1:T(8,128)(2,1)S(1)} fusion(bf16[2048,2,128]{0,2,1:T(8,128)(2,1)S(1)} %bitcast.230, f32[2,256,2048]{2,1,0:T(8,128)} %fusion.184, f32[2,256,2048]{2,1,0:T(8,128)} %get-tuple-element.70, f32[2,256]{1,0:T(2,128)} %get-tuple-element.69), kind=kOutput, calls=%fused_computation.113 | convolution fusion | flops 275843584 | bytes 9570304 | tf_op jit(solution)/shard_map/htu,uhd->thd/dot_general | solution.py:96
  434.5 8.3 %fusion.88 = bf16[256,2,128]{0,2,1:T(8,128)(2,1)S(1)} fusion(bf16[2048,2,128]{0,2,1:T(8,128)(2,1)} %bitcast.232, f32[2,256,2048]{2,1,0:T(8,128)} %fusion.181, f32[2,256,2048]{2,1,0:T(8,128)} %get-tuple-element.76, f32[2,256]{1,0:T(2,128)} %copy-done.31), kind=kOutput, calls=%fused_computation.110 | convolution fusion | flops 275843584 | bytes 9570304 | tf_op jit(solution)/shard_map/htu,uhd->thd/dot_general | solution.py:96
  443.7 9.0 %all-to-all-start.3 = ((bf16[2,128,1,1024]{1,3,2,0:T(8,128)(2,1)}), bf16[2,128,1,1024]{1,3,2,0:T(8,128)(2,1)S(1)}, u32[]{:S(2)}, u32[]{:S(2)}) async-start(bf16[2,128,1,1024]{1,3,2,0:T(8,128)(2,1)} %pad_maximum_fusion.7), calls=%async_computation.3 | async-start | bytes 1048576 | tf_op jit(solution)/shard_map/all_to_all | solution.py:37
  454.0 3.9 all-to-all-start.5
  457.9 1.1 fusion.172
  461.2 15.0 %collective-permute-done = bf16[3,2048]{0,1:T(8,128)(2,1)S(1)} collective-permute-done((bf16[3,2048]{0,1:T(8,128)(2,1)}, bf16[3,2048]{0,1:T(8,128)(2,1)S(1)}, u32[]{:S(2)}, u32[]{:S(2)}) %collective-permute-start) | collective-permute-done | bytes 12320 | tf_op jit(solution)/shard_map/ppermute | solution.py:20
  476.2 5.2 collective-permute-done.1
  481.4 5.9 fusion.138
  488.3 4.9 fusion.121
  493.4 77.0 %psum.7 = f32[7,2048]{1,0:T(8,128)} all-reduce(f32[7,2048]{1,0:T(8,128)S(1)} %stack.79), channel_id=1, replica_groups=mesh['dp'=16,'sc'=8,'core'=2] {'dp','sc','core'}, use_global_device_ids=true, to_apply=%region_27.28 | all-reduce | flops 14336 | bytes 114688 | tf_op jit(solution)/shard_map/psum | solution.py:130
  570.4 1.1 pad_maximum_fusion.10
  571.8 12.2 %reduce-scatter.19.cloned.1.call-done = bf16[256,256]{0,1:T(8,128)(2,1)} async-done(((bf16[2048,256]{0,1:T(8,128)(2,1)}), bf16[256,256]{0,1:T(8,128)(2,1)}) %reduce-scatter.19.cloned.1.call-update) | async-done | bytes 131088 | tf_op jit(solution)/shard_map/reduce_scatter | solution.py:111
  584.0 43.8 %reduce-scatter.21.cloned.1.call-done = bf16[256,256]{0,1:T(8,128)(2,1)} async-done(((bf16[2048,256]{0,1:T(8,128)(2,1)}), bf16[256,256]{0,1:T(8,128)(2,1)}) %reduce-scatter.21.cloned.1.call-update) | async-done | bytes 131088 | tf_op jit(solution)/shard_map/reduce_scatter | solution.py:111
  627.8 43.4 %reduce-scatter.23.cloned.1.call-done = bf16[256,256]{0,1:T(8,128)(2,1)} async-done(((bf16[2048,256]{0,1:T(8,128)(2,1)}), bf16[256,256]{0,1:T(8,128)(2,1)}) %reduce-scatter.23.cloned.1.call-update) | async-done | bytes 131088 | tf_op jit(solution)/shard_map/reduce_scatter | solution.py:111
  671.2 43.4 %reduce-scatter.17.cloned.1.call-done = bf16[256,256]{0,1:T(8,128)(2,1)} async-done(((bf16[2048,256]{0,1:T(8,128)(2,1)}), bf16[256,256]{0,1:T(8,128)(2,1)}) %reduce-scatter.17.cloned.1.call-update) | async-done | bytes 131088 | tf_op jit(solution)/shard_map/reduce_scatter | solution.py:111
  714.6 1.1 pad_maximum_fusion.11
  715.9 8.9 %all_to_all.83 = bf16[2,128,1,1024]{3,1,2,0:T(8,128)(2,1)S(1)} all-to-all(bf16[2,128,1,1024]{3,1,2,0:T(8,128)(2,1)S(1)} %bitcast.213), channel_id=1, replica_groups=mesh['dp'=16,'sc'=8,'core'=2] {'core'}, dimensions={0} | all-to-all | bytes 1048576 | tf_op jit(solution)/shard_map/all_to_all | solution.py:37
  725.1 1.0 copy.305
  726.1 4.1 all_to_all.84
  (170 shorter events, 27.1 us)
Async XLA Ops:
  7.2 9.7 %copy-start.9 = (bf16[1,128,2048]{2,1,0:T(8,128)(2,1)S(1)}, bf16[1,128,2048]{2,1,0:T(8,128)(2,1)}, u32[]{:S(2)}) copy-start(bf16[1,128,2048]{2,1,0:T(8,128)(2,1)} %param.7) | copy-start | bytes 1572868
  7.2 63.5 %all-gather.15.cloned.1.call-start = ((), (), s32[]{:S(2)}) async-start(), calls=%async_computation.19 | async-start | bytes 1179648 | tf_op jit(solution)/shard_map/all_gather | solution.py:76
  15.9 9.9 %copy-start.10 = (bf16[1,128,2048]{2,1,0:T(8,128)(2,1)S(1)}, bf16[1,128,2048]{2,1,0:T(8,128)(2,1)}, u32[]{:S(2)}) copy-start(bf16[1,128,2048]{2,1,0:T(8,128)(2,1)} %param.5) | copy-start | bytes 1572868
  16.8 88.1 %all-gather.13.cloned.1.call-start = ((), (), s32[]{:S(2)}) async-start(), calls=%async_computation.18 | async-start | bytes 1179648 | tf_op jit(solution)/shard_map/all_gather | solution.py:77
  17.2 13.6 %copy-start.6 = (bf16[1,128,2048]{2,1,0:T(8,128)(2,1)S(1)}, bf16[1,128,2048]{2,1,0:T(8,128)(2,1)}, u32[]{:S(2)}) copy-start(bf16[1,128,2048]{2,1,0:T(8,128)(2,1)} %param.8) | copy-start | bytes 1572868
  22.6 11.4 %copy-start.24 = (f32[7,2048]{1,0:T(8,128)S(1)}, f32[7,2048]{1,0:T(8,128)}, u32[]{:S(2)}) copy-start(f32[7,2048]{1,0:T(8,128)} %param.9) | copy-start | bytes 172036
  22.6 125.2 %all-gather.19.cloned.1.call-start = ((), (), s32[]{:S(2)}) async-start(), calls=%async_computation.21 | async-start | bytes 1179648 | tf_op jit(solution)/shard_map/all_gather | solution.py:76
  23.3 167.5 %all-gather.17.cloned.1.call-start = ((), (), s32[]{:S(2)}) async-start(), calls=%async_computation.20 | async-start | bytes 1179648 | tf_op jit(solution)/shard_map/all_gather | solution.py:77
  23.9 209.6 %all-gather.23.cloned.1.call-start = ((), (), s32[]{:S(2)}) async-start(), calls=%async_computation.23 | async-start | bytes 1179648 | tf_op jit(solution)/shard_map/all_gather | solution.py:76
  24.5 252.1 %all-gather.21.cloned.1.call-start = ((), (), s32[]{:S(2)}) async-start(), calls=%async_computation.22 | async-start | bytes 1179648 | tf_op jit(solution)/shard_map/all_gather | solution.py:77
  25.1 294.4 %all-gather.11.cloned.1.call-start = ((), (), s32[]{:S(2)}) async-start(), calls=%async_computation.17 | async-start | bytes 1179648 | tf_op jit(solution)/shard_map/all_gather | solution.py:76
  27.0 8.8 %all-to-all-start.1 = ((bf16[2,128,1,1024]{1,3,2,0:T(8,128)(2,1)}), bf16[2,128,1,1024]{1,3,2,0:T(8,128)(2,1)S(1)}, u32[]{:S(2)}, u32[]{:S(2)}) async-start(bf16[2,128,1,1024]{1,3,2,0:T(8,128)(2,1)} %pad_maximum_fusion.5), calls=%async_computation.1 | async-start | bytes 1048576 | tf_op jit(solution)/shard_map/all_to_all | solution.py:29
  30.8 332.2 %all-gather.9.cloned.1.call-start = ((), (), s32[]{:S(2)}) async-start(), calls=%async_computation.16 | async-start | bytes 1179648 | tf_op jit(solution)/shard_map/all_gather | solution.py:77
  32.1 26.1 %collective-permute-start.2 = (bf16[3,2048]{0,1:T(8,128)(2,1)}, bf16[3,2048]{0,1:T(8,128)(2,1)S(1)}, u32[]{:S(2)}, u32[]{:S(2)}) collective-permute-start(bf16[3,2048]{0,1:T(8,128)(2,1)} %get-tuple-element.40), channel_id=1, source_target_pairs={{1,0},{2,1},{3,2},{4,3},{5,4},{6,5},{7,6},{8,7},{9,8},{10,9},{11,1... | collective-permute-start | bytes 36872 | tf_op jit(solution)/shard_map/ppermute | solution.py:21
  32.2 27.0 %collective-permute-start.3 = (bf16[3,2048]{0,1:T(8,128)(2,1)S(1)}, bf16[3,2048]{0,1:T(8,128)(2,1)}, u32[]{:S(2)}, u32[]{:S(2)}) collective-permute-start(bf16[3,2048]{0,1:T(8,128)(2,1)S(1)} %get-tuple-element.41), channel_id=1, source_target_pairs={{0,1},{1,2},{2,3},{3,4},{4,5},{5,6},{6,7},{7,8},{8,9},{9,10},{10,1... | collective-permute-start | bytes 36872 | tf_op jit(solution)/shard_map/ppermute | solution.py:20
  33.9 536.5 %reduce-scatter.11.cloned.1.call-start = ((), (), s32[]{:S(2)}) async-start(), calls=%async_computation.25 | async-start | bytes 1179648 | tf_op jit(solution)/shard_map/reduce_scatter | solution.py:103
  72.2 44.0 %copy-start.7 = (bf16[2048,256]{0,1:T(8,128)(2,1)}, bf16[2048,256]{0,1:T(8,128)(2,1)S(1)}, u32[]{:S(2)}) copy-start(bf16[2048,256]{0,1:T(8,128)(2,1)S(1)} %copy.256) | copy-start | bytes 3145732
  116.2 9.9 %copy-start.12 = (bf16[256,256]{1,0:T(8,128)(2,1)S(1)}, bf16[256,256]{1,0:T(8,128)(2,1)}, u32[]{:S(2)}) copy-start(bf16[256,256]{1,0:T(8,128)(2,1)} %get-tuple-element.50) | copy-start | bytes 393220
  116.2 10.7 %copy-start.13 = (bf16[256,256]{1,0:T(8,128)(2,1)S(1)}, bf16[256,256]{1,0:T(8,128)(2,1)}, u32[]{:S(2)}) copy-start(bf16[256,256]{1,0:T(8,128)(2,1)} %get-tuple-element.36) | copy-start | bytes 393220
  125.9 444.5 %reduce-scatter.13.cloned.1.call-start = ((), (), s32[]{:S(2)}) async-start(), calls=%async_computation.26 | async-start | bytes 1179648 | tf_op jit(solution)/shard_map/reduce_scatter | solution.py:103
  192.4 10.5 %copy-start = (bf16[2048,256]{0,1:T(8,128)(2,1)}, bf16[2048,256]{0,1:T(8,128)(2,1)S(1)}, u32[]{:S(2)}) copy-start(bf16[2048,256]{0,1:T(8,128)(2,1)S(1)} %copy.259) | copy-start | bytes 3145732
  202.9 10.6 %copy-start.11 = (bf16[256,256]{1,0:T(8,128)(2,1)S(1)}, bf16[256,256]{1,0:T(8,128)(2,1)}, u32[]{:S(2)}) copy-start(bf16[256,256]{1,0:T(8,128)(2,1)} %get-tuple-element.35) | copy-start | bytes 393220
  212.6 357.8 %reduce-scatter.15.cloned.1.call-start = ((), (), s32[]{:S(2)}) async-start(), calls=%async_computation.27 | async-start | bytes 1179648 | tf_op jit(solution)/shard_map/reduce_scatter | solution.py:103
  278.1 9.7 %copy-start.2 = (bf16[2048,256]{0,1:T(8,128)(2,1)}, bf16[2048,256]{0,1:T(8,128)(2,1)S(1)}, u32[]{:S(2)}) copy-start(bf16[2048,256]{0,1:T(8,128)(2,1)S(1)} %copy.264) | copy-start | bytes 3145732
  297.5 272.9 %reduce-scatter.9.cloned.1.call-start = ((), (), s32[]{:S(2)}) async-start(), calls=%async_computation.24 | async-start | bytes 1179648 | tf_op jit(solution)/shard_map/reduce_scatter | solution.py:103
  298.6 68.6 %copy-start.16 = (bf16[256,256]{0,1:T(8,128)(2,1)}, bf16[256,256]{0,1:T(8,128)(2,1)S(1)}, u32[]{:S(2)}) copy-start(bf16[256,256]{0,1:T(8,128)(2,1)S(1)} %copy.279) | copy-start | bytes 393220
  321.8 45.4 %copy-start.18 = (bf16[256,256]{0,1:T(8,128)(2,1)S(1)}, bf16[256,256]{0,1:T(8,128)(2,1)}, u32[]{:S(2)}) copy-start(bf16[256,256]{0,1:T(8,128)(2,1)} %copy.246) | copy-start | bytes 393220
  364.5 9.0 %copy-start.4 = (bf16[2048,256]{0,1:T(8,128)(2,1)}, bf16[2048,256]{0,1:T(8,128)(2,1)S(1)}, u32[]{:S(2)}) copy-start(bf16[2048,256]{0,1:T(8,128)(2,1)S(1)} %copy.241) | copy-start | bytes 3145732
  373.5 9.7 %copy-start.31 = (f32[2,256]{1,0:T(2,128)}, f32[2,256]{1,0:T(2,128)S(1)}, u32[]{:S(2)}) copy-start(f32[2,256]{1,0:T(2,128)S(1)} %get-tuple-element.75) | copy-start | bytes 6148
  373.5 9.7 %copy-start.14 = (bf16[256,256]{0,1:T(8,128)(2,1)S(1)}, bf16[256,256]{0,1:T(8,128)(2,1)}, u32[]{:S(2)}) copy-start(bf16[256,256]{0,1:T(8,128)(2,1)} %copy.282) | copy-start | bytes 393220
  373.5 9.8 %copy-start.26 = (f32[2,256]{1,0:T(2,128)S(1)}, f32[2,256]{1,0:T(2,128)}, u32[]{:S(2)}) copy-start(f32[2,256]{1,0:T(2,128)} %get-tuple-element.73) | copy-start | bytes 6148
  383.2 4.0 copy-start.15
  383.2 4.0 copy-start.28
  383.2 200.8 %reduce-scatter.19.cloned.1.call-start = ((), (), s32[]{:S(2)}) async-start(), calls=%async_computation.29 | async-start | bytes 1179648 | tf_op jit(solution)/shard_map/reduce_scatter | solution.py:111
  386.9 240.8 %reduce-scatter.21.cloned.1.call-start = ((), (), s32[]{:S(2)}) async-start(), calls=%async_computation.30 | async-start | bytes 1179648 | tf_op jit(solution)/shard_map/reduce_scatter | solution.py:111
  387.2 3.8 copy-start.27
  391.0 280.2 %reduce-scatter.23.cloned.1.call-start = ((), (), s32[]{:S(2)}) async-start(), calls=%async_computation.31 | async-start | bytes 1179648 | tf_op jit(solution)/shard_map/reduce_scatter | solution.py:111
  394.2 8.4 %copy-start.1 = (bf16[2048,256]{0,1:T(8,128)(2,1)S(1)}, bf16[2048,256]{0,1:T(8,128)(2,1)}, u32[]{:S(2)}) copy-start(bf16[2048,256]{0,1:T(8,128)(2,1)} %copy-done) | copy-start | bytes 3145732
  402.6 3.2 copy-start.29
  409.6 8.5 %copy-start.3 = (bf16[2048,256]{0,1:T(8,128)(2,1)S(1)}, bf16[2048,256]{0,1:T(8,128)(2,1)}, u32[]{:S(2)}) copy-start(bf16[2048,256]{0,1:T(8,128)(2,1)} %copy-done.2) | copy-start | bytes 3145732
  409.6 8.5 %copy-start.30 = (f32[2,256]{1,0:T(2,128)S(1)}, f32[2,256]{1,0:T(2,128)}, u32[]{:S(2)}) copy-start(f32[2,256]{1,0:T(2,128)} %get-tuple-element.69) | copy-start | bytes 6148
  409.6 305.0 %reduce-scatter.17.cloned.1.call-start = ((), (), s32[]{:S(2)}) async-start(), calls=%async_computation.28 | async-start | bytes 1179648 | tf_op jit(solution)/shard_map/reduce_scatter | solution.py:111
  418.1 3.2 copy-start.17
  418.1 3.2 copy-start.32
  421.4 3.9 copy-start.5
  421.4 3.9 copy-start.25
  425.2 1.2 copy-start.8
  443.7 37.7 %copy-start.19 = (f32[1,2048]{1,0:T(1,128)S(1)}, f32[1,2048]{1,0:T(1,128)}, u32[]{:S(2)}) copy-start(f32[1,2048]{1,0:T(1,128)} %get-tuple-element.64) | copy-start | bytes 24580
  443.7 37.7 %copy-start.20 = (f32[1,2048]{1,0:T(1,128)S(1)}, f32[1,2048]{1,0:T(1,128)}, u32[]{:S(2)}) copy-start(f32[1,2048]{1,0:T(1,128)} %get-tuple-element.65) | copy-start | bytes 24580
  443.7 37.7 %copy-start.21 = (f32[1,2048]{1,0:T(1,128)S(1)}, f32[1,2048]{1,0:T(1,128)}, u32[]{:S(2)}) copy-start(f32[1,2048]{1,0:T(1,128)} %get-tuple-element.66) | copy-start | bytes 24580
  443.7 37.7 %copy-start.22 = (f32[1,2048]{1,0:T(1,128)S(1)}, f32[1,2048]{1,0:T(1,128)}, u32[]{:S(2)}) copy-start(f32[1,2048]{1,0:T(1,128)} %get-tuple-element.67) | copy-start | bytes 24580
  443.7 37.7 %copy-start.23 = (f32[1,2048]{1,0:T(1,128)S(1)}, f32[1,2048]{1,0:T(1,128)}, u32[]{:S(2)}) copy-start(f32[1,2048]{1,0:T(1,128)} %get-tuple-element.68) | copy-start | bytes 24580
  443.7 10.3 %all-to-all-start.3 = ((bf16[2,128,1,1024]{1,3,2,0:T(8,128)(2,1)}), bf16[2,128,1,1024]{1,3,2,0:T(8,128)(2,1)S(1)}, u32[]{:S(2)}, u32[]{:S(2)}) async-start(bf16[2,128,1,1024]{1,3,2,0:T(8,128)(2,1)} %pad_maximum_fusion.7), calls=%async_computation.3 | async-start | bytes 1048576 | tf_op jit(solution)/shard_map/all_to_all | solution.py:37
  454.0 6.1 all-to-all-start.5
  459.0 17.2 %collective-permute-start = (bf16[3,2048]{0,1:T(8,128)(2,1)}, bf16[3,2048]{0,1:T(8,128)(2,1)S(1)}, u32[]{:S(2)}, u32[]{:S(2)}) collective-permute-start(bf16[3,2048]{0,1:T(8,128)(2,1)} %bitcast.31), channel_id=1, source_target_pairs={{0,1},{1,2},{2,3},{3,4},{4,5},{5,6},{6,7},{7,8},{8,9},{9,10},{10,1... | collective-permute-start | bytes 36872 | tf_op jit(solution)/shard_map/ppermute | solution.py:20
  459.0 22.4 %collective-permute-start.1 = (bf16[3,2048]{0,1:T(8,128)(2,1)}, bf16[3,2048]{0,1:T(8,128)(2,1)}, u32[]{:S(2)}, u32[]{:S(2)}) collective-permute-start(bf16[3,2048]{0,1:T(8,128)(2,1)} %bitcast.39), channel_id=1, source_target_pairs={{1,0},{2,1},{3,2},{4,3},{5,4},{6,5},{7,6},{8,7},{9,8},{10,9},{11,1... | collective-permute-start | bytes 36872 | tf_op jit(solution)/shard_map/ppermute | solution.py:21
Sparse Core Ops, SparseCore 0:
  16.9 46.0 all-gather.14
  64.8 40.0 all-gather.12
  106.7 41.0 all-gather.18
  149.4 41.3 all-gather.16
  192.5 40.9 all-gather.22
  235.1 41.4 all-gather.20
  278.4 41.0 all-gather.10
  321.9 41.1 all-gather.8
  365.6 41.2 reduce-scatter.10
  409.2 41.2 reduce-scatter.12
  453.0 42.6 reduce-scatter.14
  498.1 42.3 reduce-scatter.8
  543.0 40.8 reduce-scatter.18
  586.4 41.3 reduce-scatter.20
  630.1 40.9 reduce-scatter.22
  673.6 40.9 reduce-scatter.16
